TPU v7x, 128 devices: a whole 4x4x4 slice. The times are simulated.
128 devices in a mesh: ctx: 8 (over x, y_hi), head: 16 (over y_lo, z, core).
Axes of the slice: x: 4, y: 4 (y_hi: 2, y_lo: 2; y = y_hi * 2 + y_lo), z: 4, core: 2. Of those that a mesh axis runs over, the one named last changes fastest.
Arguments:
- hidden_in: bfloat16 [8192, 5376], P(('ctx', 'head')), may hold values from -6 to 6
- pre_gain: float32 [5376], replicated, may hold values from 0.1 to 1.9
- w_query: bfloat16 [5376, 4096], P('ctx', 'head'), may hold values from -0.054554473 to 0.054554473, as said below
- w_key: bfloat16 [5376, 2048], P('ctx', 'head'), may hold values from -0.054554473 to 0.054554473, as said below
- value_weight: bfloat16 [5376, 2048], P('ctx', 'head'), may hold values from -0.078125 to 0.078125
- query_gain: float32 [128], replicated, may hold values from 0.6 to 7, as said below
- key_norm_gain: float32 [128], replicated, may hold values from 0.6 to 7, as said below
- w_output: bfloat16 [4096, 5376], P(('head', 'ctx')), may hold values from -0.09375 to 0.09375
- post_gain: float32 [5376], replicated, may hold values from 0.1 to 1.9
Outputs:
- layer_out: bfloat16 [8192, 5376], P(('ctx', 'head'))
Inputs may be any that keep to these rules, and one draw needn't show every extreme that they name: `w_query`: entries are normal draws clipped to 4 standard deviations, scaled by 5376 ** -0.5. `w_key`: entries are normal draws clipped to 4 standard deviations, scaled by 5376 ** -0.5. `query_gain`: positive gains. `key_norm_gain`: positive gains.
All inputs are finite; a program needn't handle non-finite values.
Results may differ from a plain program's by a relative error of at most 0.015.
The roundings to bfloat16 on the way count: a program that leaves them out, or rounds other values in their place, can miss the bound.
Values may be sent and summed in bfloat16 or wider, within the bound.
No kernel may reach another device: no remote copies, remote signals or barrier semaphores. Data moves between devices by JAX's collectives and lax.ppermute only.
A program may use at most 64 MiB of HBM per device.

v0:
```python
import jax
import jax.numpy as jnp
from jax import lax
from jax.sharding import Mesh, PartitionSpec as P

HEAD_SIZE = 128
WINDOW_SPAN = 1024
norm_eps = 1e-06
query_scale = 168.0 ** (-0.5)
rope_base = 10000.0
mask_value = -1e30
CTX = ("cx", "cy")
HEAD = ("hc", "core")


def passed_along(shard, axis, by):
    count = lax.axis_size(axis)
    pairs = [(i, i + by) for i in range(count) if 0 <= i + by < count]
    return lax.ppermute(shard, axis, pairs)


def rotated(shard, axis, by):
    count = lax.axis_size(axis)
    pairs = [(i, (i + by) % count) for i in range(count)]
    return lax.ppermute(shard, axis, pairs)


def placed(parts, me, count):
    stacked = jnp.zeros((count,) + parts[0].shape, parts[0].dtype)
    for i, part in enumerate(parts):
        stacked = lax.dynamic_update_index_in_dim(stacked, part, (me + i) % count, 0)
    return stacked


def ring_over_cx(piece):
    half = piece.shape[0] // 2
    from_left = rotated(piece, "cx", 1)
    from_right = rotated(piece, "cx", -1)
    far = jnp.concatenate(
        [rotated(from_left[:half], "cx", 1), rotated(from_right[half:], "cx", -1)]
    )
    return [piece, from_right, far, from_left]


def gathered_over_ctx(piece):
    cy = lax.axis_index("cy")
    cx = lax.axis_index("cx")
    own = ring_over_cx(piece)
    partner = ring_over_cx(rotated(piece, "cy", 1))
    pairs = [placed([a, b], cy, 2) for a, b in zip(own, partner)]
    ring = placed(pairs, cx, 4)
    return ring.reshape((8 * piece.shape[0],) + piece.shape[1:])


def root_mean_scale(values, scaling):
    mean_sq = jnp.mean(values * values, axis=-1, keepdims=True)
    return values * lax.rsqrt(mean_sq + norm_eps) * scaling


def apply_rotary(values, token_places):
    full_width = values.shape[-1]
    half_width = full_width // 2
    frequency = rope_base ** (-jnp.arange(half_width, dtype=jnp.float32) * 2.0 / full_width)
    angles = token_places.astype(jnp.float32)[:, None] * frequency[None, :]
    cosine = jnp.cos(angles)[:, None, :]
    sine_part = jnp.sin(angles)[:, None, :]
    lower_half = values[..., :half_width]
    upper_half = values[..., half_width:]
    return jnp.concatenate(
        [
            lower_half * cosine - upper_half * sine_part,
            upper_half * cosine + lower_half * sine_part,
        ],
        axis=-1,
    )


def body(
    hidden_in,
    pre_gain,
    w_query,
    w_key,
    value_weight,
    query_gain,
    key_norm_gain,
    w_output,
    post_gain,
):
    own_rows = hidden_in.astype(jnp.float32)
    q_cols = w_query.shape[1]
    k_cols = w_key.shape[1]
    w_in = gathered_over_ctx(jnp.concatenate([w_query, w_key, value_weight], axis=1))
    own_normed = root_mean_scale(own_rows, pre_gain).astype(jnp.bfloat16)
    normed = lax.all_gather(own_normed, HEAD, axis=0, tiled=True)
    normed, w_output = lax.optimization_barrier((normed, w_output))
    out_weight = gathered_over_ctx(w_output)
    tok_count = normed.shape[0]
    projected = jnp.dot(normed, w_in, preferred_element_type=jnp.float32)
    query_raw = projected[:, :q_cols]
    key_unnormed = projected[:, q_cols : q_cols + k_cols]
    value_unnormed = projected[:, q_cols + k_cols :]
    local_heads = q_cols // HEAD_SIZE
    local_groups = k_cols // HEAD_SIZE
    heads_per_group = local_heads // local_groups
    ctx_index = lax.axis_index(CTX)
    token_places = ctx_index * tok_count + jnp.arange(tok_count, dtype=jnp.int32)
    query_matrix = (
        apply_rotary(
            root_mean_scale(query_raw.reshape(tok_count, local_heads, HEAD_SIZE), query_gain),
            token_places,
        )
        * query_scale
    ).astype(jnp.bfloat16)
    projected_keys = apply_rotary(
        root_mean_scale(key_unnormed.reshape(tok_count, local_groups, HEAD_SIZE), key_norm_gain),
        token_places,
    ).astype(jnp.bfloat16)
    projected_values = value_unnormed.astype(jnp.bfloat16)
    key_value = jnp.stack(
        [projected_keys.reshape(tok_count, local_groups * HEAD_SIZE), projected_values]
    )
    pieces = [passed_along(key_value, CTX, 1)]
    extended = jnp.concatenate(pieces + [key_value], axis=1)
    band_keys = extended[0].reshape(-1, local_groups, HEAD_SIZE)
    band_values = extended[1].reshape(-1, local_groups, HEAD_SIZE)
    block_rows = min(512, tok_count)
    grouped_queries = query_matrix.reshape(tok_count, local_groups, heads_per_group, HEAD_SIZE)
    outputs = []
    for block_index in range(tok_count // block_rows):
        first_row = block_index * block_rows
        query_block = grouped_queries[first_row : first_row + block_rows]
        key_block = band_keys[first_row : first_row + block_rows + WINDOW_SPAN]
        value_block = band_values[first_row : first_row + block_rows + WINDOW_SPAN]
        scores = jnp.einsum(
            "qjgd,kjd->jgqk", query_block, key_block, preferred_element_type=jnp.float32
        )
        query_spots = token_places[first_row : first_row + block_rows]
        key_spots = (
            ctx_index * tok_count
            - WINDOW_SPAN
            + first_row
            + jnp.arange(block_rows + WINDOW_SPAN, dtype=jnp.int32)
        )
        allowed = (
            (key_spots[None, :] <= query_spots[:, None])
            & (key_spots[None, :] > query_spots[:, None] - WINDOW_SPAN)
            & (key_spots[None, :] >= 0)
        )
        scores = jnp.where(allowed, scores, mask_value)
        row_max = jnp.max(scores, axis=-1, keepdims=True)
        weights = jnp.exp(scores - row_max)
        row_sum = jnp.sum(weights, axis=-1, keepdims=True)
        probabilities = (weights / row_sum).astype(jnp.bfloat16)
        mixed = jnp.einsum(
            "jgqk,kjd->qjgd", probabilities, value_block, preferred_element_type=jnp.float32
        )
        outputs.append(mixed.astype(jnp.bfloat16).reshape(block_rows, local_heads * HEAD_SIZE))
    attended = jnp.concatenate(outputs, axis=0)
    partial_value = jnp.dot(attended, out_weight, preferred_element_type=jnp.float32).astype(
        jnp.bfloat16
    )
    summed = lax.psum_scatter(partial_value, HEAD, scatter_dimension=0, tiled=True).astype(
        jnp.float32
    )
    result = own_rows + root_mean_scale(summed, post_gain)
    return result.astype(jnp.bfloat16)


def solution(mesh):
    ctx_size, head_size = mesh.devices.shape
    view = Mesh(mesh.devices.reshape(ctx_size // 2, 2, head_size // 2, 2), CTX + HEAD)
    rows_spec = P(CTX + HEAD, None)
    cols_spec = P(CTX, HEAD)
    return jax.shard_map(
        body,
        mesh=view,
        in_specs=(
            rows_spec,
            P(),
            cols_spec,
            cols_spec,
            cols_spec,
            P(),
            P(),
            P(HEAD + CTX, None),
            P(),
        ),
        out_specs=rows_spec,
        check_vma=False,
    )
```

profile of v0, /device:TPU:0, one launch (start us, length us, event | category | flops | bytes accessed | tf_op | source)
XLA Modules:
  0.0 240.7 jit_solution(18410239072865604457)
XLA Ops:
  8.0 2.2 fusion.12
  12.4 3.3 %collective-permute-start = (bf16[672,512]{1,0:T(8,128)(2,1)}, bf16[672,512]{1,0:T(8,128)(2,1)}, u32[]{:S(2)}, u32[]{:S(2)}) collective-permute-start(bf16[672,512]{1,0:T(8,128)(2,1)} %constant_dynamic-update-slice_fusion), channel_id=1, source_target_pairs={{0,16},{16,0},{1,17},{17,1},{2,18},{18,2},{3,19},{19,3},{4,20},{20... | collective-permute-start | bytes 2064392 | tf_op jit(solution)/shard_map/ppermute | solution.py:25
  15.7 2.8 %collective-permute-start.1 = (bf16[672,512]{1,0:T(8,128)(2,1)}, bf16[672,512]{1,0:T(8,128)(2,1)}, u32[]{:S(2)}, u32[]{:S(2)}) collective-permute-start(bf16[672,512]{1,0:T(8,128)(2,1)} %constant_dynamic-update-slice_fusion), channel_id=1, source_target_pairs={{0,96},{32,0},{64,32},{96,64},{1,97},{33,1},{65,33},{97,65},{2,98}... | collective-permute-start | bytes 2064392 | tf_op jit(solution)/shard_map/ppermute | solution.py:25
  21.0 2.9 %multiply_cosine_fusion = (f32[1024,64]{1,0:T(8,128)S(1)}, f32[1024,64]{1,0:T(8,128)}) fusion(f32[64]{0:T(128)S(1)} %multiply_power_fusion, f32[1024]{0:T(1024)S(1)} %get-tuple-element.24), kind=kLoop, calls=%fused_computation.38 | loop fusion | flops 65536 | bytes 528640 | tf_op jit(solution)/shard_map/cos | solution.py:65
  25.0 11.5 %collective-permute-done.3 = bf16[672,512]{1,0:T(8,128)(2,1)S(1)} collective-permute-done((bf16[672,512]{1,0:T(8,128)(2,1)}, bf16[672,512]{1,0:T(8,128)(2,1)S(1)}, u32[]{:S(2)}, u32[]{:S(2)}) %collective-permute-start.3) | collective-permute-done | bytes 688160 | tf_op jit(solution)/shard_map/ppermute | solution.py:25
  37.7 3.3 %collective-permute-start.5 = (bf16[336,512]{1,0:T(8,128)(2,1)S(1)}, bf16[336,512]{1,0:T(8,128)(2,1)S(1)}, u32[]{:S(2)}, u32[]{:S(2)}) collective-permute-start(bf16[336,512]{1,0:T(8,128)(2,1)S(1)} %slice.106), channel_id=1, source_target_pairs={{0,96},{32,0},{64,32},{96,64},{1,97},{33,1},{65,33},{97,65},{2,98}... | collective-permute-start | bytes 1032200 | tf_op jit(solution)/shard_map/ppermute | solution.py:25
  40.9 2.4 %collective-permute-start.2 = (bf16[672,512]{1,0:T(8,128)(2,1)}, bf16[672,512]{1,0:T(8,128)(2,1)S(1)}, u32[]{:S(2)}, u32[]{:S(2)}) collective-permute-start(bf16[672,512]{1,0:T(8,128)(2,1)} %collective-permute-done), channel_id=1, source_target_pairs={{0,96},{32,0},{64,32},{96,64},{1,97},{33,1},{65,33},{97,65},{2,98}... | collective-permute-start | bytes 2064392 | tf_op jit(solution)/shard_map/ppermute | solution.py:25
  45.8 2.8 %broadcast_in_dim.112 = bf16[4,2,672,512]{3,2,1,0:T(8,128)(2,1)} broadcast(bf16[]{:T(256)} %constant.186.clone.1), dimensions={} | broadcast | bytes 5505026 | tf_op jit(solution)/shard_map/broadcast_in_dim | solution.py:29
  50.1 10.9 %collective-permute-done.6 = bf16[672,512]{1,0:T(8,128)(2,1)S(1)} collective-permute-done((bf16[672,512]{1,0:T(8,128)(2,1)}, bf16[672,512]{1,0:T(8,128)(2,1)S(1)}, u32[]{:S(2)}, u32[]{:S(2)}) %collective-permute-start.6) | collective-permute-done | bytes 688160 | tf_op jit(solution)/shard_map/ppermute | solution.py:25
  61.6 3.7 %collective-permute-start.8 = (bf16[336,512]{1,0:T(8,128)(2,1)S(1)}, bf16[336,512]{1,0:T(8,128)(2,1)S(1)}, u32[]{:S(2)}, u32[]{:S(2)}) collective-permute-start(bf16[336,512]{1,0:T(8,128)(2,1)S(1)} %slice.108), channel_id=1, source_target_pairs={{0,96},{32,0},{64,32},{96,64},{1,97},{33,1},{65,33},{97,65},{2,98}... | collective-permute-start | bytes 1032200 | tf_op jit(solution)/shard_map/ppermute | solution.py:25
  66.6 3.4 %collective-permute-done.7 = bf16[336,512]{1,0:T(8,128)(2,1)S(1)} collective-permute-done((bf16[336,512]{1,0:T(8,128)(2,1)S(1)}, bf16[336,512]{1,0:T(8,128)(2,1)S(1)}, u32[]{:S(2)}, u32[]{:S(2)}) %collective-permute-start.7) | collective-permute-done | bytes 344096 | tf_op jit(solution)/shard_map/ppermute | solution.py:25
  72.5 12.5 %all-gather.2.cloned.1.call-done = bf16[1024,5376]{1,0:T(8,128)(2,1)} async-done(((bf16[64,5376]{1,0:T(8,128)(2,1)}), bf16[1024,5376]{1,0:T(8,128)(2,1)}) %all-gather.2.cloned.1.call-update) | async-done | bytes 11010064 | tf_op jit(solution)/shard_map/all_gather | solution.py:94
  85.0 10.3 %fusion.48 = f32[1024,512]{0,1:T(8,128)S(1)} fusion(bf16[1024,5376]{1,0:T(8,128)(2,1)} %all-gather.2.cloned.1.call-done, bf16[5376,512]{1,0:T(8,128)(2,1)} %bitcast.8), kind=kOutput, calls=%fused_computation.115 | convolution fusion | flops 5637144576 | bytes 18612224 | tf_op jit(solution)/shard_map/dot_general | solution.py:98
  96.6 1.9 collective-permute-start.10
  98.6 2.8 %collective-permute-start.11 = (bf16[32,5376]{1,0:T(8,128)(2,1)}, bf16[32,5376]{1,0:T(8,128)(2,1)}, u32[]{:S(2)}, u32[]{:S(2)}) collective-permute-start(bf16[32,5376]{1,0:T(8,128)(2,1)} %param.16), channel_id=1, source_target_pairs={{0,96},{32,0},{64,32},{96,64},{1,97},{33,1},{65,33},{97,65},{2,98}... | collective-permute-start | bytes 1032200 | tf_op jit(solution)/shard_map/ppermute | solution.py:25
  103.5 4.4 %collective-permute-start.9 = (bf16[2,1024,128]{1,2,0:T(8,128)(2,1)}, bf16[2,1024,128]{1,2,0:T(8,128)(2,1)}, u32[]{:S(2)}, u32[]{:S(2)}) collective-permute-start(bf16[2,1024,128]{1,2,0:T(8,128)(2,1)} %pad_maximum_fusion), channel_id=1, source_target_pairs={{0,16},{16,32},{32,48},{48,64},{64,80},{80,96},{96,112},{1,17},{17... | collective-permute-start | bytes 1572872 | tf_op jit(solution)/shard_map/ppermute | solution.py:19
  114.4 3.3 %collective-permute-start.15 = (bf16[16,5376]{1,0:T(8,128)(2,1)S(1)}, bf16[16,5376]{1,0:T(8,128)(2,1)S(1)}, u32[]{:S(2)}, u32[]{:S(2)}) collective-permute-start(bf16[16,5376]{1,0:T(8,128)(2,1)S(1)} %slice.123), channel_id=1, source_target_pairs={{0,96},{32,0},{64,32},{96,64},{1,97},{33,1},{65,33},{97,65},{2,98}... | collective-permute-start | bytes 516104 | tf_op jit(solution)/shard_map/ppermute | solution.py:25
  127.5 2.0 fusion.14
  132.2 2.0 fusion.17
  135.5 2.4 %collective-permute-start.18 = (bf16[16,5376]{1,0:T(8,128)(2,1)S(1)}, bf16[16,5376]{1,0:T(8,128)(2,1)S(1)}, u32[]{:S(2)}, u32[]{:S(2)}) collective-permute-start(bf16[16,5376]{1,0:T(8,128)(2,1)S(1)} %slice.125), channel_id=1, source_target_pairs={{0,96},{32,0},{64,32},{96,64},{1,97},{33,1},{65,33},{97,65},{2,98}... | collective-permute-start | bytes 516104 | tf_op jit(solution)/shard_map/ppermute | solution.py:25
  138.0 2.9 %collective-permute-done.17 = bf16[16,5376]{1,0:T(8,128)(2,1)S(1)} collective-permute-done((bf16[16,5376]{1,0:T(8,128)(2,1)S(1)}, bf16[16,5376]{1,0:T(8,128)(2,1)S(1)}, u32[]{:S(2)}, u32[]{:S(2)}) %collective-permute-start.17) | collective-permute-done | bytes 172064 | tf_op jit(solution)/shard_map/ppermute | solution.py:25
  141.3 5.9 %convolution_convert_fusion = bf16[1024,5376]{1,0:T(8,128)(2,1)} fusion(bf16[256,5376]{1,0:T(8,128)(2,1)S(1)} %bitcast.131, bf16[512,256]{0,1:T(8,128)(2,1)S(1)} %bitcast.134, bf16[512,256]{0,1:T(8,128)(2,1)S(1)} %bitcast.133), kind=kOutput, calls=%fused_computation | convolution fusion | flops 2825125888 | bytes 14286848 | tf_op jit(solution)/shard_map/dot_general | solution.py:159
  147.2 83.0 %reduce-scatter.2.cloned.1.call-done = bf16[64,5376]{1,0:T(8,128)(2,1)} async-done(((bf16[1024,5376]{1,0:T(8,128)(2,1)}), bf16[64,5376]{1,0:T(8,128)(2,1)}) %reduce-scatter.2.cloned.1.call-update) | async-done | bytes 688144 | tf_op jit(solution)/shard_map/reduce_scatter | solution.py:162
  231.6 2.3 fusion.13
  (122 shorter events, 41.8 us)
Async XLA Ops:
  6.5 78.5 %all-gather.2.cloned.1.call-start = ((), (), s32[]{:S(2)}) async-start(), calls=%async_computation.1 | async-start | bytes 11698176 | tf_op jit(solution)/shard_map/all_gather | solution.py:94
  10.2 220.1 %reduce-scatter.2.cloned.1.call-start = ((), (), s32[]{:S(2)}) async-start(), calls=%async_computation.2 | async-start | bytes 11698176 | tf_op jit(solution)/shard_map/reduce_scatter | solution.py:162
  12.4 28.5 %collective-permute-start = (bf16[672,512]{1,0:T(8,128)(2,1)}, bf16[672,512]{1,0:T(8,128)(2,1)}, u32[]{:S(2)}, u32[]{:S(2)}) collective-permute-start(bf16[672,512]{1,0:T(8,128)(2,1)} %constant_dynamic-update-slice_fusion), channel_id=1, source_target_pairs={{0,16},{16,0},{1,17},{17,1},{2,18},{18,2},{3,19},{19,3},{4,20},{20... | collective-permute-start | bytes 2064392 | tf_op jit(solution)/shard_map/ppermute | solution.py:25
  15.7 20.9 %collective-permute-start.1 = (bf16[672,512]{1,0:T(8,128)(2,1)}, bf16[672,512]{1,0:T(8,128)(2,1)}, u32[]{:S(2)}, u32[]{:S(2)}) collective-permute-start(bf16[672,512]{1,0:T(8,128)(2,1)} %constant_dynamic-update-slice_fusion), channel_id=1, source_target_pairs={{0,96},{32,0},{64,32},{96,64},{1,97},{33,1},{65,33},{97,65},{2,98}... | collective-permute-start | bytes 2064392 | tf_op jit(solution)/shard_map/ppermute | solution.py:25
  18.5 18.0 %collective-permute-start.3 = (bf16[672,512]{1,0:T(8,128)(2,1)}, bf16[672,512]{1,0:T(8,128)(2,1)S(1)}, u32[]{:S(2)}, u32[]{:S(2)}) collective-permute-start(bf16[672,512]{1,0:T(8,128)(2,1)} %constant_dynamic-update-slice_fusion), channel_id=1, source_target_pairs={{0,32},{32,64},{64,96},{96,0},{1,33},{33,65},{65,97},{97,1},{2,34}... | collective-permute-start | bytes 2064392 | tf_op jit(solution)/shard_map/ppermute | solution.py:25
  36.6 13.4 %collective-permute-start.4 = (bf16[336,512]{1,0:T(8,128)(2,1)S(1)}, bf16[336,512]{1,0:T(8,128)(2,1)S(1)}, u32[]{:S(2)}, u32[]{:S(2)}) collective-permute-start(bf16[336,512]{1,0:T(8,128)(2,1)S(1)} %slice.105), channel_id=1, source_target_pairs={{0,32},{32,64},{64,96},{96,0},{1,33},{33,65},{65,97},{97,1},{2,34}... | collective-permute-start | bytes 1032200 | tf_op jit(solution)/shard_map/ppermute | solution.py:25
  37.7 12.3 %collective-permute-start.5 = (bf16[336,512]{1,0:T(8,128)(2,1)S(1)}, bf16[336,512]{1,0:T(8,128)(2,1)S(1)}, u32[]{:S(2)}, u32[]{:S(2)}) collective-permute-start(bf16[336,512]{1,0:T(8,128)(2,1)S(1)} %slice.106), channel_id=1, source_target_pairs={{0,96},{32,0},{64,32},{96,64},{1,97},{33,1},{65,33},{97,65},{2,98}... | collective-permute-start | bytes 1032200 | tf_op jit(solution)/shard_map/ppermute | solution.py:25
  40.9 20.6 %collective-permute-start.2 = (bf16[672,512]{1,0:T(8,128)(2,1)}, bf16[672,512]{1,0:T(8,128)(2,1)S(1)}, u32[]{:S(2)}, u32[]{:S(2)}) collective-permute-start(bf16[672,512]{1,0:T(8,128)(2,1)} %collective-permute-done), channel_id=1, source_target_pairs={{0,96},{32,0},{64,32},{96,64},{1,97},{33,1},{65,33},{97,65},{2,98}... | collective-permute-start | bytes 2064392 | tf_op jit(solution)/shard_map/ppermute | solution.py:25
  43.4 17.7 %collective-permute-start.6 = (bf16[672,512]{1,0:T(8,128)(2,1)}, bf16[672,512]{1,0:T(8,128)(2,1)S(1)}, u32[]{:S(2)}, u32[]{:S(2)}) collective-permute-start(bf16[672,512]{1,0:T(8,128)(2,1)} %collective-permute-done), channel_id=1, source_target_pairs={{0,32},{32,64},{64,96},{96,0},{1,33},{33,65},{65,97},{97,1},{2,34}... | collective-permute-start | bytes 2064392 | tf_op jit(solution)/shard_map/ppermute | solution.py:25
  61.1 8.9 %collective-permute-start.7 = (bf16[336,512]{1,0:T(8,128)(2,1)S(1)}, bf16[336,512]{1,0:T(8,128)(2,1)S(1)}, u32[]{:S(2)}, u32[]{:S(2)}) collective-permute-start(bf16[336,512]{1,0:T(8,128)(2,1)S(1)} %slice.107), channel_id=1, source_target_pairs={{0,32},{32,64},{64,96},{96,0},{1,33},{33,65},{65,97},{97,1},{2,34}... | collective-permute-start | bytes 1032200 | tf_op jit(solution)/shard_map/ppermute | solution.py:25
  61.6 8.5 %collective-permute-start.8 = (bf16[336,512]{1,0:T(8,128)(2,1)S(1)}, bf16[336,512]{1,0:T(8,128)(2,1)S(1)}, u32[]{:S(2)}, u32[]{:S(2)}) collective-permute-start(bf16[336,512]{1,0:T(8,128)(2,1)S(1)} %slice.108), channel_id=1, source_target_pairs={{0,96},{32,0},{64,32},{96,64},{1,97},{33,1},{65,33},{97,65},{2,98}... | collective-permute-start | bytes 1032200 | tf_op jit(solution)/shard_map/ppermute | solution.py:25
  96.6 21.1 %collective-permute-start.10 = (bf16[32,5376]{1,0:T(8,128)(2,1)}, bf16[32,5376]{1,0:T(8,128)(2,1)}, u32[]{:S(2)}, u32[]{:S(2)}) collective-permute-start(bf16[32,5376]{1,0:T(8,128)(2,1)} %param.16), channel_id=1, source_target_pairs={{0,16},{16,0},{1,17},{17,1},{2,18},{18,2},{3,19},{19,3},{4,20},{20... | collective-permute-start | bytes 1032200 | tf_op jit(solution)/shard_map/ppermute | solution.py:25
  98.6 14.9 %collective-permute-start.11 = (bf16[32,5376]{1,0:T(8,128)(2,1)}, bf16[32,5376]{1,0:T(8,128)(2,1)}, u32[]{:S(2)}, u32[]{:S(2)}) collective-permute-start(bf16[32,5376]{1,0:T(8,128)(2,1)} %param.16), channel_id=1, source_target_pairs={{0,96},{32,0},{64,32},{96,64},{1,97},{33,1},{65,33},{97,65},{2,98}... | collective-permute-start | bytes 1032200 | tf_op jit(solution)/shard_map/ppermute | solution.py:25
  101.3 11.2 %collective-permute-start.13 = (bf16[32,5376]{1,0:T(8,128)(2,1)}, bf16[32,5376]{1,0:T(8,128)(2,1)}, u32[]{:S(2)}, u32[]{:S(2)}) collective-permute-start(bf16[32,5376]{1,0:T(8,128)(2,1)} %param.16), channel_id=1, source_target_pairs={{0,32},{32,64},{64,96},{96,0},{1,33},{33,65},{65,97},{97,1},{2,34}... | collective-permute-start | bytes 1032200 | tf_op jit(solution)/shard_map/ppermute | solution.py:25
  101.4 9.1 %copy-start.9 = (f32[128]{0:T(128)S(1)}, f32[128]{0:T(128)}, u32[]{:S(2)}) copy-start(f32[128]{0:T(128)} %param.14) | copy-start | bytes 1540
  103.5 19.8 %collective-permute-start.9 = (bf16[2,1024,128]{1,2,0:T(8,128)(2,1)}, bf16[2,1024,128]{1,2,0:T(8,128)(2,1)}, u32[]{:S(2)}, u32[]{:S(2)}) collective-permute-start(bf16[2,1024,128]{1,2,0:T(8,128)(2,1)} %pad_maximum_fusion), channel_id=1, source_target_pairs={{0,16},{16,32},{32,48},{48,64},{64,80},{80,96},{96,112},{1,17},{17... | collective-permute-start | bytes 1572872 | tf_op jit(solution)/shard_map/ppermute | solution.py:19
  113.4 9.8 %collective-permute-start.14 = (bf16[16,5376]{1,0:T(8,128)(2,1)S(1)}, bf16[16,5376]{1,0:T(8,128)(2,1)S(1)}, u32[]{:S(2)}, u32[]{:S(2)}) collective-permute-start(bf16[16,5376]{1,0:T(8,128)(2,1)S(1)} %slice.122), channel_id=1, source_target_pairs={{0,32},{32,64},{64,96},{96,0},{1,33},{33,65},{65,97},{97,1},{2,34}... | collective-permute-start | bytes 516104 | tf_op jit(solution)/shard_map/ppermute | solution.py:25
  114.4 8.8 %collective-permute-start.15 = (bf16[16,5376]{1,0:T(8,128)(2,1)S(1)}, bf16[16,5376]{1,0:T(8,128)(2,1)S(1)}, u32[]{:S(2)}, u32[]{:S(2)}) collective-permute-start(bf16[16,5376]{1,0:T(8,128)(2,1)S(1)} %slice.123), channel_id=1, source_target_pairs={{0,96},{32,0},{64,32},{96,64},{1,97},{33,1},{65,33},{97,65},{2,98}... | collective-permute-start | bytes 516104 | tf_op jit(solution)/shard_map/ppermute | solution.py:25
  117.7 17.7 %collective-permute-start.12 = (bf16[32,5376]{1,0:T(8,128)(2,1)}, bf16[32,5376]{1,0:T(8,128)(2,1)S(1)}, u32[]{:S(2)}, u32[]{:S(2)}) collective-permute-start(bf16[32,5376]{1,0:T(8,128)(2,1)} %collective-permute-done.10), channel_id=1, source_target_pairs={{0,96},{32,0},{64,32},{96,64},{1,97},{33,1},{65,33},{97,65},{2,98}... | collective-permute-start | bytes 1032200 | tf_op jit(solution)/shard_map/ppermute | solution.py:25
  118.3 15.9 %collective-permute-start.16 = (bf16[32,5376]{1,0:T(8,128)(2,1)}, bf16[32,5376]{1,0:T(8,128)(2,1)S(1)}, u32[]{:S(2)}, u32[]{:S(2)}) collective-permute-start(bf16[32,5376]{1,0:T(8,128)(2,1)} %collective-permute-done.10), channel_id=1, source_target_pairs={{0,32},{32,64},{64,96},{96,0},{1,33},{33,65},{65,97},{97,1},{2,34}... | collective-permute-start | bytes 1032200 | tf_op jit(solution)/shard_map/ppermute | solution.py:25
  134.2 6.7 %collective-permute-start.17 = (bf16[16,5376]{1,0:T(8,128)(2,1)S(1)}, bf16[16,5376]{1,0:T(8,128)(2,1)S(1)}, u32[]{:S(2)}, u32[]{:S(2)}) collective-permute-start(bf16[16,5376]{1,0:T(8,128)(2,1)S(1)} %slice.124), channel_id=1, source_target_pairs={{0,32},{32,64},{64,96},{96,0},{1,33},{33,65},{65,97},{97,1},{2,34}... | collective-permute-start | bytes 516104 | tf_op jit(solution)/shard_map/ppermute | solution.py:25
  135.5 5.7 %collective-permute-start.18 = (bf16[16,5376]{1,0:T(8,128)(2,1)S(1)}, bf16[16,5376]{1,0:T(8,128)(2,1)S(1)}, u32[]{:S(2)}, u32[]{:S(2)}) collective-permute-start(bf16[16,5376]{1,0:T(8,128)(2,1)S(1)} %slice.125), channel_id=1, source_target_pairs={{0,96},{32,0},{64,32},{96,64},{1,97},{33,1},{65,33},{97,65},{2,98}... | collective-permute-start | bytes 516104 | tf_op jit(solution)/shard_map/ppermute | solution.py:25
  147.2 84.4 %copy-start = (bf16[64,5376]{1,0:T(8,128)(2,1)S(1)}, bf16[64,5376]{1,0:T(8,128)(2,1)}, u32[]{:S(2)}) copy-start(bf16[64,5376]{1,0:T(8,128)(2,1)} %param.9) | copy-start | bytes 2064388
  147.2 84.4 %copy-start.7 = (f32[5376]{0:T(1024)S(1)}, f32[5376]{0:T(1024)}, u32[]{:S(2)}) copy-start(f32[5376]{0:T(1024)} %param.17) | copy-start | bytes 64516
  (7 other events, 27.0 us)
Sparse Core Ops, SparseCore 0:
  10.3 74.6 all-gather.1
  147.4 82.8 reduce-scatter.1
where the time goes:
time: 241 us
  waiting for transfers between devices  126 us (52%)
  starting transfers between devices  33.8 us (14%)
  local copies, waits for them, and re-layouts  24.7 us (10%)
  matrix products  22.8 us (9%)
  other arithmetic  19.8 us (8%)
  between operations  14 us (6%)
    reduce_scatter x1, waiting for transfers between devices, body(): lax.psum_scatter(partial_value, HEAD, scatter_dimension=0, tiled=True)  83 us
    ppermute x18, waiting for transfers between devices, rotated(): return lax.ppermute(shard, axis, pairs)  30.2 us
    ppermute x18, starting transfers between devices, rotated(): return lax.ppermute(shard, axis, pairs)  29.3 us
    dynamic_update_slice x20, local copies, waits for them, and re-layouts, placed(): lax.dynamic_update_index_in_dim(stacked, part, (me + i) % count, 0)  12.8 us
    all_gather x1, waiting for transfers between devices, body(): normed = lax.all_gather(own_normed, HEAD, axis=0, tiled=True)  12.5 us
    dot_general x1, matrix products, body(): projected = jnp.dot(normed, w_in, preferred_element_type=jnp.float32)  10.3 us
    dot_general x1, matrix products, body(): jnp.dot(attended, out_weight, preferred_element_type=jnp.float32)  5.86 us
  transfers between devices with their start and end apart: 21, of which 10 were waited for; matrix products, arithmetic and copies ran while one was open for 17% of the time, Pallas kernels for 0%

commit v1 on v0

--- a/solution.py
+++ b/solution.py
@@ -91,7 +91,9 @@
     k_cols = w_key.shape[1]
     w_in = gathered_over_ctx(jnp.concatenate([w_query, w_key, value_weight], axis=1))
     own_normed = root_mean_scale(own_rows, pre_gain).astype(jnp.bfloat16)
-    normed = lax.all_gather(own_normed, HEAD, axis=0, tiled=True)
+    normed = jnp.concatenate(
+        lax.all_to_all(jnp.stack([own_normed] * lax.axis_size(HEAD)), HEAD, 0, 0), axis=0
+    )
     normed, w_output = lax.optimization_barrier((normed, w_output))
     out_weight = gathered_over_ctx(w_output)
     tok_count = normed.shape[0]

time: 241 us -> 392 us (1.63)
  waiting for transfers between devices: 126 us -> 265 us
  starting transfers between devices: 33.8 us -> 41.9 us
  local copies, waits for them, and re-layouts: 24.7 us -> 29.4 us
    ppermute x18, waiting for transfers between devices: 30.2 us -> 184 us  [rotated(): return lax.ppermute(shard, axis, pairs)]
    all_gather x1 -> x0, waiting for transfers between devices: 12.5 us -> none  [body(): normed = lax.all_gather(own_normed, HEAD, axis=0, tiled=True)]
    all_to_all x0 -> x1, starting transfers between devices: none -> 6.72 us  [body(): lax.all_to_all(jnp.stack([own_normed] * lax.axis_size(HEAD)), HEAD, 0, 0)]
    another operation x0 -> x1, local copies, waits for them, and re-layouts: none -> 5.09 us  [body(): jnp.stack([own_normed] * lax.axis_size(HEAD))]
  transfers between devices with their start and end apart: 21 -> 21, of which waited for: 10 -> 6; matrix products, arithmetic and copies ran while one was open for 17% -> 11% of each run, Pallas kernels for 0% -> 0%
where the time goes in v1:
time: 392 us
  waiting for transfers between devices  265 us (68%)
  starting transfers between devices  41.9 us (11%)
  local copies, waits for them, and re-layouts  29.4 us (8%)
  matrix products  22.8 us (6%)
  other arithmetic  18.9 us (5%)
  between operations  14 us (4%)
    ppermute x18, waiting for transfers between devices, rotated(): return lax.ppermute(shard, axis, pairs)  184 us
    reduce_scatter x1, waiting for transfers between devices, body(): lax.psum_scatter(partial_value, HEAD, scatter_dimension=0, tiled=True)  80.3 us
    ppermute x18, starting transfers between devices, rotated(): return lax.ppermute(shard, axis, pairs)  29.6 us
    dynamic_update_slice x20, local copies, waits for them, and re-layouts, placed(): lax.dynamic_update_index_in_dim(stacked, part, (me + i) % count, 0)  12.8 us
    dot_general x1, matrix products, body(): projected = jnp.dot(normed, w_in, preferred_element_type=jnp.float32)  10.3 us
  transfers between devices with their start and end apart: 21, of which 6 were waited for; matrix products, arithmetic and copies ran while one was open for 11% of the time, Pallas kernels for 0%

profile of v1, /device:TPU:0, one launch (start us, length us, event | category | flops | bytes accessed | tf_op | source)
XLA Modules:
  0.0 391.6 jit_solution(7319361529158923659)
XLA Ops:
  9.2 5.1 %stack.6 = bf16[16,64,5376]{2,1,0:T(8,128)(2,1)} broadcast(bf16[64,5376]{1,0:T(8,128)(2,1)S(1)} %fusion.12), dimensions={1,2} | broadcast | bytes 11698176 | tf_op jit(solution)/shard_map/stack | solution.py:95
  14.3 6.7 %all-to-all-start = ((bf16[16,64,5376]{2,1,0:T(8,128)(2,1)}), bf16[16,64,5376]{2,1,0:T(8,128)(2,1)}, u32[]{:S(2)}, u32[]{:S(2)}) async-start(bf16[16,64,5376]{2,1,0:T(8,128)(2,1)} %stack.6), calls=%async_computation | async-start | bytes 22020096 | tf_op jit(solution)/shard_map/all_to_all | solution.py:95
  23.2 2.9 collective-permute-start
  26.1 2.8 collective-permute-start.1
  31.4 2.9 multiply_cosine_fusion
  35.4 12.0 %collective-permute-done.3 = bf16[672,512]{1,0:T(8,128)(2,1)S(1)} collective-permute-done((bf16[672,512]{1,0:T(8,128)(2,1)}, bf16[672,512]{1,0:T(8,128)(2,1)S(1)}, u32[]{:S(2)}, u32[]{:S(2)}) %collective-permute-start.3) | collective-permute-done | bytes 688160 | tf_op jit(solution)/shard_map/ppermute | solution.py:25
  48.6 3.3 collective-permute-start.5
  51.9 152.7 %collective-permute-done = bf16[672,512]{1,0:T(8,128)(2,1)} collective-permute-done((bf16[672,512]{1,0:T(8,128)(2,1)}, bf16[672,512]{1,0:T(8,128)(2,1)}, u32[]{:S(2)}, u32[]{:S(2)}) %collective-permute-start) | collective-permute-done | bytes 688160 | tf_op jit(solution)/shard_map/ppermute | solution.py:25
  204.5 2.8 collective-permute-start.2
  209.7 2.9 broadcast_in_dim.112
  214.2 11.5 %collective-permute-done.6 = bf16[672,512]{1,0:T(8,128)(2,1)S(1)} collective-permute-done((bf16[672,512]{1,0:T(8,128)(2,1)}, bf16[672,512]{1,0:T(8,128)(2,1)S(1)}, u32[]{:S(2)}, u32[]{:S(2)}) %collective-permute-start.6) | collective-permute-done | bytes 688160 | tf_op jit(solution)/shard_map/ppermute | solution.py:25
  225.9 3.5 collective-permute-start.8
  230.6 5.2 %collective-permute-done.7 = bf16[336,512]{1,0:T(8,128)(2,1)S(1)} collective-permute-done((bf16[336,512]{1,0:T(8,128)(2,1)S(1)}, bf16[336,512]{1,0:T(8,128)(2,1)S(1)}, u32[]{:S(2)}, u32[]{:S(2)}) %collective-permute-start.7) | collective-permute-done | bytes 344096 | tf_op jit(solution)/shard_map/ppermute | solution.py:25
  238.3 10.3 %fusion.48 = f32[1024,512]{0,1:T(8,128)S(1)} fusion(bf16[1024,5376]{1,0:T(8,128)(2,1)} %bitcast, bf16[5376,512]{1,0:T(8,128)(2,1)} %bitcast.9), kind=kOutput, calls=%fused_computation.115 | convolution fusion | flops 5637144576 | bytes 18612224 | tf_op jit(solution)/shard_map/dot_general | solution.py:100
  250.0 3.3 collective-permute-start.11
  256.1 5.6 %collective-permute-start.9 = (bf16[2,1024,128]{1,2,0:T(8,128)(2,1)}, bf16[2,1024,128]{1,2,0:T(8,128)(2,1)}, u32[]{:S(2)}, u32[]{:S(2)}) collective-permute-start(bf16[2,1024,128]{1,2,0:T(8,128)(2,1)} %pad_maximum_fusion), channel_id=1, source_target_pairs={{0,16},{16,32},{32,48},{48,64},{64,80},{80,96},{96,112},{1,17},{17... | collective-permute-start | bytes 1572872 | tf_op jit(solution)/shard_map/ppermute | solution.py:19
  267.6 3.3 collective-permute-start.15
  272.2 3.2 collective-permute-start.12
  286.1 2.0 fusion.17
  288.2 3.5 collective-permute-start.18
  291.9 2.9 collective-permute-done.17
  295.0 5.9 %convolution_convert_fusion = bf16[1024,5376]{1,0:T(8,128)(2,1)} fusion(bf16[256,5376]{1,0:T(8,128)(2,1)S(1)} %bitcast.132, bf16[512,256]{0,1:T(8,128)(2,1)S(1)} %bitcast.135, bf16[512,256]{0,1:T(8,128)(2,1)S(1)} %bitcast.134), kind=kOutput, calls=%fused_computation | convolution fusion | flops 2825125888 | bytes 14286848 | tf_op jit(solution)/shard_map/dot_general | solution.py:161
  300.9 80.3 %reduce-scatter.2.cloned.1.call-done = bf16[64,5376]{1,0:T(8,128)(2,1)} async-done(((bf16[1024,5376]{1,0:T(8,128)(2,1)}), bf16[64,5376]{1,0:T(8,128)(2,1)}) %reduce-scatter.2.cloned.1.call-update) | async-done | bytes 688144 | tf_op jit(solution)/shard_map/reduce_scatter | solution.py:164
  382.5 2.3 fusion.13
  (122 shorter events, 40.8 us)
Async XLA Ops:
  14.3 224.0 %all-to-all-start = ((bf16[16,64,5376]{2,1,0:T(8,128)(2,1)}), bf16[16,64,5376]{2,1,0:T(8,128)(2,1)}, u32[]{:S(2)}, u32[]{:S(2)}) async-start(bf16[16,64,5376]{2,1,0:T(8,128)(2,1)} %stack.6), calls=%async_computation | async-start | bytes 22020096 | tf_op jit(solution)/shard_map/all_to_all | solution.py:95
  21.0 360.1 %reduce-scatter.2.cloned.1.call-start = ((), (), s32[]{:S(2)}) async-start(), calls=%async_computation.2 | async-start | bytes 11698176 | tf_op jit(solution)/shard_map/reduce_scatter | solution.py:164
  23.2 181.3 %collective-permute-start = (bf16[672,512]{1,0:T(8,128)(2,1)}, bf16[672,512]{1,0:T(8,128)(2,1)}, u32[]{:S(2)}, u32[]{:S(2)}) collective-permute-start(bf16[672,512]{1,0:T(8,128)(2,1)} %constant_dynamic-update-slice_fusion), channel_id=1, source_target_pairs={{0,16},{16,0},{1,17},{17,1},{2,18},{18,2},{3,19},{19,3},{4,20},{20... | collective-permute-start | bytes 2064392 | tf_op jit(solution)/shard_map/ppermute | solution.py:25
  26.1 21.4 %collective-permute-start.1 = (bf16[672,512]{1,0:T(8,128)(2,1)}, bf16[672,512]{1,0:T(8,128)(2,1)}, u32[]{:S(2)}, u32[]{:S(2)}) collective-permute-start(bf16[672,512]{1,0:T(8,128)(2,1)} %constant_dynamic-update-slice_fusion), channel_id=1, source_target_pairs={{0,96},{32,0},{64,32},{96,64},{1,97},{33,1},{65,33},{97,65},{2,98}... | collective-permute-start | bytes 2064392 | tf_op jit(solution)/shard_map/ppermute | solution.py:25
  28.9 18.6 %collective-permute-start.3 = (bf16[672,512]{1,0:T(8,128)(2,1)}, bf16[672,512]{1,0:T(8,128)(2,1)S(1)}, u32[]{:S(2)}, u32[]{:S(2)}) collective-permute-start(bf16[672,512]{1,0:T(8,128)(2,1)} %constant_dynamic-update-slice_fusion), channel_id=1, source_target_pairs={{0,32},{32,64},{64,96},{96,0},{1,33},{33,65},{65,97},{97,1},{2,34}... | collective-permute-start | bytes 2064392 | tf_op jit(solution)/shard_map/ppermute | solution.py:25
  47.5 166.5 %collective-permute-start.4 = (bf16[336,512]{1,0:T(8,128)(2,1)S(1)}, bf16[336,512]{1,0:T(8,128)(2,1)S(1)}, u32[]{:S(2)}, u32[]{:S(2)}) collective-permute-start(bf16[336,512]{1,0:T(8,128)(2,1)S(1)} %slice.105), channel_id=1, source_target_pairs={{0,32},{32,64},{64,96},{96,0},{1,33},{33,65},{65,97},{97,1},{2,34}... | collective-permute-start | bytes 1032200 | tf_op jit(solution)/shard_map/ppermute | solution.py:25
  48.6 165.4 %collective-permute-start.5 = (bf16[336,512]{1,0:T(8,128)(2,1)S(1)}, bf16[336,512]{1,0:T(8,128)(2,1)S(1)}, u32[]{:S(2)}, u32[]{:S(2)}) collective-permute-start(bf16[336,512]{1,0:T(8,128)(2,1)S(1)} %slice.106), channel_id=1, source_target_pairs={{0,96},{32,0},{64,32},{96,64},{1,97},{33,1},{65,33},{97,65},{2,98}... | collective-permute-start | bytes 1032200 | tf_op jit(solution)/shard_map/ppermute | solution.py:25
  204.5 21.3 %collective-permute-start.2 = (bf16[672,512]{1,0:T(8,128)(2,1)}, bf16[672,512]{1,0:T(8,128)(2,1)S(1)}, u32[]{:S(2)}, u32[]{:S(2)}) collective-permute-start(bf16[672,512]{1,0:T(8,128)(2,1)} %collective-permute-done), channel_id=1, source_target_pairs={{0,96},{32,0},{64,32},{96,64},{1,97},{33,1},{65,33},{97,65},{2,98}... | collective-permute-start | bytes 2064392 | tf_op jit(solution)/shard_map/ppermute | solution.py:25
  207.3 18.4 %collective-permute-start.6 = (bf16[672,512]{1,0:T(8,128)(2,1)}, bf16[672,512]{1,0:T(8,128)(2,1)S(1)}, u32[]{:S(2)}, u32[]{:S(2)}) collective-permute-start(bf16[672,512]{1,0:T(8,128)(2,1)} %collective-permute-done), channel_id=1, source_target_pairs={{0,32},{32,64},{64,96},{96,0},{1,33},{33,65},{65,97},{97,1},{2,34}... | collective-permute-start | bytes 2064392 | tf_op jit(solution)/shard_map/ppermute | solution.py:25
  225.7 10.0 %collective-permute-start.7 = (bf16[336,512]{1,0:T(8,128)(2,1)S(1)}, bf16[336,512]{1,0:T(8,128)(2,1)S(1)}, u32[]{:S(2)}, u32[]{:S(2)}) collective-permute-start(bf16[336,512]{1,0:T(8,128)(2,1)S(1)} %slice.107), channel_id=1, source_target_pairs={{0,32},{32,64},{64,96},{96,0},{1,33},{33,65},{65,97},{97,1},{2,34}... | collective-permute-start | bytes 1032200 | tf_op jit(solution)/shard_map/ppermute | solution.py:25
  225.9 9.9 %collective-permute-start.8 = (bf16[336,512]{1,0:T(8,128)(2,1)S(1)}, bf16[336,512]{1,0:T(8,128)(2,1)S(1)}, u32[]{:S(2)}, u32[]{:S(2)}) collective-permute-start(bf16[336,512]{1,0:T(8,128)(2,1)S(1)} %slice.108), channel_id=1, source_target_pairs={{0,96},{32,0},{64,32},{96,64},{1,97},{33,1},{65,33},{97,65},{2,98}... | collective-permute-start | bytes 1032200 | tf_op jit(solution)/shard_map/ppermute | solution.py:25
  249.9 15.7 %collective-permute-start.13 = (bf16[32,5376]{1,0:T(8,128)(2,1)}, bf16[32,5376]{1,0:T(8,128)(2,1)}, u32[]{:S(2)}, u32[]{:S(2)}) collective-permute-start(bf16[32,5376]{1,0:T(8,128)(2,1)} %param.16), channel_id=1, source_target_pairs={{0,32},{32,64},{64,96},{96,0},{1,33},{33,65},{65,97},{97,1},{2,34}... | collective-permute-start | bytes 1032200 | tf_op jit(solution)/shard_map/ppermute | solution.py:25
  250.0 16.6 %collective-permute-start.11 = (bf16[32,5376]{1,0:T(8,128)(2,1)}, bf16[32,5376]{1,0:T(8,128)(2,1)}, u32[]{:S(2)}, u32[]{:S(2)}) collective-permute-start(bf16[32,5376]{1,0:T(8,128)(2,1)} %param.16), channel_id=1, source_target_pairs={{0,96},{32,0},{64,32},{96,64},{1,97},{33,1},{65,33},{97,65},{2,98}... | collective-permute-start | bytes 1032200 | tf_op jit(solution)/shard_map/ppermute | solution.py:25
  253.3 17.6 %collective-permute-start.10 = (bf16[32,5376]{1,0:T(8,128)(2,1)}, bf16[32,5376]{1,0:T(8,128)(2,1)}, u32[]{:S(2)}, u32[]{:S(2)}) collective-permute-start(bf16[32,5376]{1,0:T(8,128)(2,1)} %param.16), channel_id=1, source_target_pairs={{0,16},{16,0},{1,17},{17,1},{2,18},{18,2},{3,19},{19,3},{4,20},{20... | collective-permute-start | bytes 1032200 | tf_op jit(solution)/shard_map/ppermute | solution.py:25
  254.0 10.4 %copy-start.9 = (f32[128]{0:T(128)S(1)}, f32[128]{0:T(128)}, u32[]{:S(2)}) copy-start(f32[128]{0:T(128)} %param.14) | copy-start | bytes 1540
  256.1 21.6 %collective-permute-start.9 = (bf16[2,1024,128]{1,2,0:T(8,128)(2,1)}, bf16[2,1024,128]{1,2,0:T(8,128)(2,1)}, u32[]{:S(2)}, u32[]{:S(2)}) collective-permute-start(bf16[2,1024,128]{1,2,0:T(8,128)(2,1)} %pad_maximum_fusion), channel_id=1, source_target_pairs={{0,16},{16,32},{32,48},{48,64},{64,80},{80,96},{96,112},{1,17},{17... | collective-permute-start | bytes 1572872 | tf_op jit(solution)/shard_map/ppermute | solution.py:19
  266.6 11.0 %collective-permute-start.14 = (bf16[16,5376]{1,0:T(8,128)(2,1)S(1)}, bf16[16,5376]{1,0:T(8,128)(2,1)S(1)}, u32[]{:S(2)}, u32[]{:S(2)}) collective-permute-start(bf16[16,5376]{1,0:T(8,128)(2,1)S(1)} %slice.122), channel_id=1, source_target_pairs={{0,32},{32,64},{64,96},{96,0},{1,33},{33,65},{65,97},{97,1},{2,34}... | collective-permute-start | bytes 516104 | tf_op jit(solution)/shard_map/ppermute | solution.py:25
  267.6 10.0 %collective-permute-start.15 = (bf16[16,5376]{1,0:T(8,128)(2,1)S(1)}, bf16[16,5376]{1,0:T(8,128)(2,1)S(1)}, u32[]{:S(2)}, u32[]{:S(2)}) collective-permute-start(bf16[16,5376]{1,0:T(8,128)(2,1)S(1)} %slice.123), channel_id=1, source_target_pairs={{0,96},{32,0},{64,32},{96,64},{1,97},{33,1},{65,33},{97,65},{2,98}... | collective-permute-start | bytes 516104 | tf_op jit(solution)/shard_map/ppermute | solution.py:25
  272.1 16.0 %collective-permute-start.16 = (bf16[32,5376]{1,0:T(8,128)(2,1)}, bf16[32,5376]{1,0:T(8,128)(2,1)S(1)}, u32[]{:S(2)}, u32[]{:S(2)}) collective-permute-start(bf16[32,5376]{1,0:T(8,128)(2,1)} %collective-permute-done.10), channel_id=1, source_target_pairs={{0,32},{32,64},{64,96},{96,0},{1,33},{33,65},{65,97},{97,1},{2,34}... | collective-permute-start | bytes 1032200 | tf_op jit(solution)/shard_map/ppermute | solution.py:25
  272.2 16.0 %collective-permute-start.12 = (bf16[32,5376]{1,0:T(8,128)(2,1)}, bf16[32,5376]{1,0:T(8,128)(2,1)S(1)}, u32[]{:S(2)}, u32[]{:S(2)}) collective-permute-start(bf16[32,5376]{1,0:T(8,128)(2,1)} %collective-permute-done.10), channel_id=1, source_target_pairs={{0,96},{32,0},{64,32},{96,64},{1,97},{33,1},{65,33},{97,65},{2,98}... | collective-permute-start | bytes 1032200 | tf_op jit(solution)/shard_map/ppermute | solution.py:25
  288.1 6.7 %collective-permute-start.17 = (bf16[16,5376]{1,0:T(8,128)(2,1)S(1)}, bf16[16,5376]{1,0:T(8,128)(2,1)S(1)}, u32[]{:S(2)}, u32[]{:S(2)}) collective-permute-start(bf16[16,5376]{1,0:T(8,128)(2,1)S(1)} %slice.124), channel_id=1, source_target_pairs={{0,32},{32,64},{64,96},{96,0},{1,33},{33,65},{65,97},{97,1},{2,34}... | collective-permute-start | bytes 516104 | tf_op jit(solution)/shard_map/ppermute | solution.py:25
  288.2 6.6 %collective-permute-start.18 = (bf16[16,5376]{1,0:T(8,128)(2,1)S(1)}, bf16[16,5376]{1,0:T(8,128)(2,1)S(1)}, u32[]{:S(2)}, u32[]{:S(2)}) collective-permute-start(bf16[16,5376]{1,0:T(8,128)(2,1)S(1)} %slice.125), channel_id=1, source_target_pairs={{0,96},{32,0},{64,32},{96,64},{1,97},{33,1},{65,33},{97,65},{2,98}... | collective-permute-start | bytes 516104 | tf_op jit(solution)/shard_map/ppermute | solution.py:25
  300.8 81.6 %copy-start = (bf16[64,5376]{1,0:T(8,128)(2,1)S(1)}, bf16[64,5376]{1,0:T(8,128)(2,1)}, u32[]{:S(2)}) copy-start(bf16[64,5376]{1,0:T(8,128)(2,1)} %param.9) | copy-start | bytes 2064388
  300.8 81.6 %copy-start.7 = (f32[5376]{0:T(1024)S(1)}, f32[5376]{0:T(1024)}, u32[]{:S(2)}) copy-start(f32[5376]{0:T(1024)} %param.17) | copy-start | bytes 64516
  (7 other events, 41.5 us)
Sparse Core Ops, SparseCore 0:
  301.0 80.0 reduce-scatter.1
